TPU v7x, 512 devices: a whole 4x4x16 slice. The times are simulated.
512 devices in a mesh: seq: 128 (over z, x, core), fsdp: 4 (over y).
Axes of the slice: x: 4, y: 4, z: 16, core: 2. Of those that a mesh axis runs over, the one named last changes fastest.
Arguments:
- query_key: bfloat16 [131072, 3072], P(('seq', 'fsdp')), may hold values from -48 to 48
- values: bfloat16 [131072, 3072], P(('seq', 'fsdp')), may hold values from -6 to 6
- cluster_ids: int32 [24, 1024], replicated, may hold values from 0 to 127, as said below
Outputs:
- attended: bfloat16 [131072, 3072], P(('seq', 'fsdp'))
Inputs may be any that keep to these rules, and one draw needn't show every extreme that they name: `cluster_ids`: for every head and cluster at most 10 blocks name that cluster, and for every head some cluster is named by exactly 10 blocks. Among the (head, block) pairs of one group of 6 consecutive heads and one run of 8 blocks starting at a multiple of 8, no cluster is named more than 1 times, and some cluster exactly 1 times; the blocks of one such run name distinct clusters for each head.
All inputs are finite; a program needn't handle non-finite values.
Results may differ from a plain program's by a relative error of at most 0.0027.
Values may be sent and summed in bfloat16 or wider, within the bound.
No kernel may reach another device: no remote copies, remote signals or barrier semaphores. Data moves between devices by JAX's collectives and lax.ppermute only.
A program may use at most 64 MiB of HBM per device.

v0:
```python
import math
import jax
import jax.numpy as jnp
from jax import lax
from jax.sharding import PartitionSpec as P

BLK = 128
masked_score = -1e30


def by_index(source_table, row_index):
    return source_table[jnp.clip(row_index, 0, source_table.shape[0] - 1)]


def softmax_group(key_rows, positions, alive_rows, score_scale):
    scores = jnp.dot(key_rows, key_rows.T, preferred_element_type=jnp.float32) * score_scale
    allowed = alive_rows[None, :] & (positions[None, :] <= positions[:, None])
    scores = jnp.where(allowed, scores, masked_score)
    row_peak = jnp.max(scores, axis=1, keepdims=True)
    weights = jnp.where(allowed, jnp.exp(scores - row_peak), 0.0)
    row_total = jnp.where(alive_rows[:, None], jnp.sum(weights, axis=1, keepdims=True), 1.0)
    return (weights.astype(jnp.bfloat16), row_total)


def shards(query_key, values, cluster_ids):
    seq_count = lax.axis_size("seq")
    group_count = lax.axis_size("fsdp")
    seq_index = lax.axis_index("seq")
    group_index = lax.axis_index("fsdp")
    heads_all = cluster_ids.shape[0]
    group_heads = heads_all // group_count
    head_dim = query_key.shape[1] // heads_all
    tok_rows = query_key.shape[0]
    shard_blocks = group_count * tok_rows // BLK
    all_blocks = cluster_ids.shape[1]
    item_count = group_heads * shard_blocks
    slot_count = max(1, item_count // seq_count)
    capacity = shard_blocks + min(shard_blocks // 4, seq_count - shard_blocks)
    group_rows = capacity * BLK
    send_rows = seq_count * slot_count
    score_scale = 1.0 / math.sqrt(head_dim)
    own_blocks = tok_rows // BLK
    keys_local = lax.all_to_all(query_key, "fsdp", split_axis=1, concat_axis=0, tiled=True)
    value_chunks = values.reshape(tok_rows, group_count, group_heads * head_dim)
    value_chunks, keys_local = lax.optimization_barrier((value_chunks, keys_local))
    by_shift = [lax.dynamic_index_in_dim(value_chunks, group_index, 1, keepdims=False)]
    for shift in range(1, group_count):
        outgoing = lax.dynamic_index_in_dim(
            value_chunks, (group_index + shift) % group_count, 1, keepdims=False
        )
        by_shift.append(
            lax.ppermute(
                outgoing,
                "fsdp",
                [(peer, (peer + shift) % group_count) for peer in range(group_count)],
            )
        )
    source_order = (group_index - jnp.arange(group_count, dtype=jnp.int32)) % group_count
    values_local = jnp.stack(by_shift)[source_order].reshape(
        group_count * tok_rows, group_heads * head_dim
    )

    def into_items(block_data):
        shaped = block_data.reshape(shard_blocks, BLK, group_heads, head_dim)
        return jnp.transpose(shaped, (2, 0, 1, 3)).reshape(item_count, BLK, head_dim)

    key_items = into_items(keys_local)
    value_items = into_items(values_local)
    group_ids = lax.dynamic_slice_in_dim(cluster_ids, group_index * group_heads, group_heads, 0)
    by_source = jnp.transpose(
        group_ids.reshape(group_heads, seq_count, shard_blocks), (1, 0, 2)
    ).reshape(seq_count, item_count)
    own_dest = lax.dynamic_index_in_dim(by_source, seq_index, 0, keepdims=False)
    item_ids = jnp.arange(item_count, dtype=jnp.int32)
    earlier = (own_dest[None, :] == own_dest[:, None]) & (item_ids[None, :] < item_ids[:, None])
    own_pos = own_dest * slot_count + jnp.sum(earlier.astype(jnp.int32), axis=1)
    row_ids = jnp.arange(send_rows, dtype=jnp.int32)
    slot_match = own_pos[None, :] == row_ids[:, None]
    send_pick = jnp.sum(jnp.where(slot_match, item_ids[None, :], 0), axis=1) + item_count * (
        1 - jnp.any(slot_match, axis=1).astype(jnp.int32)
    )
    key_send, group_ids = lax.optimization_barrier((by_index(key_items, send_pick), group_ids))
    arrived_k = lax.all_to_all(key_send, "seq", split_axis=0, concat_axis=0, tiled=True)
    value_send = by_index(value_items, send_pick)
    arrived_k, value_send = lax.optimization_barrier((arrived_k, value_send))
    arrived_v = lax.all_to_all(value_send, "seq", split_axis=0, concat_axis=0, tiled=True)
    by_source = jnp.transpose(
        group_ids.reshape(group_heads, seq_count, shard_blocks), (1, 0, 2)
    ).reshape(seq_count, item_count)
    received_mask = (by_source == seq_index).astype(jnp.int32)
    recv_pos = (
        jnp.arange(seq_count, dtype=jnp.int32)[:, None] * slot_count
        + jnp.cumsum(received_mask, axis=1)
        - received_mask
    )
    recv_by_head = jnp.transpose(
        recv_pos.reshape(seq_count, group_heads, shard_blocks), (1, 0, 2)
    ).reshape(group_heads * all_blocks)
    owned_mask = (group_ids == seq_index).astype(jnp.int32)
    ordinal = jnp.cumsum(owned_mask, axis=1) - owned_mask
    target = jnp.where(
        owned_mask > 0, jnp.arange(group_heads, dtype=jnp.int32)[:, None] * capacity + ordinal, -1
    ).reshape(group_heads * all_blocks)
    slot_ids = jnp.arange(group_heads * capacity, dtype=jnp.int32)
    matches = target[None, :] == slot_ids[:, None]
    present = jnp.any(matches, axis=1)
    source_row = jnp.sum(jnp.where(matches, recv_by_head[None, :], 0), axis=1) + send_rows * (
        1 - present.astype(jnp.int32)
    )
    block_ids = jnp.tile(jnp.arange(all_blocks, dtype=jnp.int32), group_heads)
    block_of = jnp.sum(jnp.where(matches, block_ids[None, :], 0), axis=1)
    key_grouped = by_index(arrived_k, source_row)
    value_grouped = by_index(arrived_v, source_row)
    positions = (block_of[:, None] * BLK + jnp.arange(BLK, dtype=jnp.int32)[None, :]).reshape(
        group_heads, group_rows
    )
    alive_rows = jnp.repeat(present, BLK).reshape(group_heads, group_rows)

    def one_head(operands):
        key_rows, where_at, alive_here = operands
        return softmax_group(key_rows, where_at, alive_here, score_scale)

    weights, totals = lax.map(
        one_head, (key_grouped.reshape(group_heads, group_rows, head_dim), positions, alive_rows)
    )
    value_rows = value_grouped.reshape(group_heads, group_rows, head_dim)
    back_match = source_row[None, :] == row_ids[:, None]
    back_pick = jnp.sum(
        jnp.where(back_match, slot_ids[None, :], 0), axis=1
    ) + group_heads * capacity * (1 - jnp.any(back_match, axis=1).astype(jnp.int32))
    weighted = jnp.einsum("hqk,hkd->hqd", weights, value_rows, preferred_element_type=jnp.float32)
    outputs = (
        (weighted / totals).astype(jnp.bfloat16).reshape(group_heads * capacity, BLK, head_dim)
    )
    returned = lax.all_to_all(
        by_index(outputs, back_pick), "seq", split_axis=0, concat_axis=0, tiled=True
    )
    own_output = by_index(returned, own_pos).reshape(
        group_heads, group_count, own_blocks, BLK, head_dim
    )
    gathered = lax.all_to_all(
        jnp.swapaxes(own_output, 0, 1), "fsdp", split_axis=0, concat_axis=0, tiled=True
    )
    token_major = jnp.transpose(gathered, (2, 3, 0, 1, 4))
    return token_major.reshape(tok_rows, heads_all * head_dim)


def solution(mesh):
    placed = (P(("seq", "fsdp"), None), P(("seq", "fsdp"), None), P())
    return jax.shard_map(
        shards, mesh=mesh, in_specs=placed, out_specs=P(("seq", "fsdp"), None), check_vma=False
    )
```

profile of v0, /device:TPU:70, one launch (start us, length us, event | category | flops | bytes accessed | tf_op | source)
XLA Modules:
  0.0 684.2 jit_solution(3121798839654760957)
XLA Ops:
  0.0 2.6 copy.60
  2.6 4.6 all-to-all-start
  7.2 1.0 reshape.313
  8.2 1.1 copy.64
  9.3 0.2 dynamic-slice_reduce_fusion.2
  9.5 0.2 convert_reduce_fusion
  9.8 1.6 copy.59
  11.8 16.1 %all-to-all-done = bf16[256,4,768]{0,2,1:T(8,128)(2,1)S(1)} async-done(((bf16[256,4,768]{0,2,1:T(8,128)(2,1)}), bf16[256,4,768]{0,2,1:T(8,128)(2,1)S(1)}, u32[]{:S(2)}, u32[]{:S(2)}) %all-to-all-start) | async-done | bytes 1572896 | tf_op jit(solution)/shard_map/all_to_all | solution.py:43
  27.9 0.7 copy.61
  28.6 0.8 copy.62
  29.4 0.4 copy.86
  29.8 1.1 copy.63
  31.0 3.1 gather_fusion
  34.1 18.9 %all-to-all-start.1 = ((bf16[128,128,128]{2,1,0:T(8,128)(2,1)}), bf16[128,128,128]{2,1,0:T(8,128)(2,1)}, u32[]{:S(2)}, u32[]{:S(2)}) async-start(bf16[128,128,128]{2,1,0:T(8,128)(2,1)} %gather_fusion), calls=%async_computation.1 | async-start | bytes 8388608 | tf_op jit(solution)/shard_map/all_to_all | solution.py:83
  53.3 1.7 reduce-window.6
  55.0 0.2 slice_reduce_fusion
  55.5 0.2 reshape.334
  56.2 0.2 broadcast_in_dim.121
  56.7 2.5 collective-permute-start
  59.4 4.0 collective-permute-start.1
  63.5 2.5 collective-permute-start.2
  66.3 0.6 select_reduce_fusion
  67.0 0.3 fusion.9
  67.9 11.5 %collective-permute-done = bf16[256,768]{1,0:T(8,128)(2,1)S(1)} collective-permute-done((bf16[256,768]{1,0:T(8,128)(2,1)S(1)}, bf16[256,768]{1,0:T(8,128)(2,1)S(1)}, u32[]{:S(2)}, u32[]{:S(2)}) %collective-permute-start) | collective-permute-done | bytes 393248 | tf_op jit(solution)/shard_map/ppermute | solution.py:52
  79.4 2.7 collective-permute-done.2
  82.1 0.7 copy-done.4
  82.9 1.2 pad_maximum_fusion
  84.0 0.6 gather_fusion.1
  84.7 1.0 copy.72
  85.8 0.6 reshape_reshape.4
  86.4 1.1 copy.73
  87.5 3.1 gather_fusion.2
  90.7 150.5 %all-to-all-done.1 = bf16[128,128,128]{2,1,0:T(8,128)(2,1)} async-done(((bf16[128,128,128]{2,1,0:T(8,128)(2,1)}), bf16[128,128,128]{2,1,0:T(8,128)(2,1)}, u32[]{:S(2)}, u32[]{:S(2)}) %all-to-all-start.1) | async-done | bytes 4194336 | tf_op jit(solution)/shard_map/all_to_all | solution.py:83
  241.2 8.9 %all-to-all-start.2 = ((bf16[128,128,128]{2,1,0:T(8,128)(2,1)}), bf16[128,128,128]{2,1,0:T(8,128)(2,1)}, u32[]{:S(2)}, u32[]{:S(2)}) async-start(bf16[128,128,128]{2,1,0:T(8,128)(2,1)} %gather_fusion.2), calls=%async_computation.2 | async-start | bytes 8388608 | tf_op jit(solution)/shard_map/all_to_all | solution.py:86
  250.2 3.1 gather_fusion.3
  253.3 46.0 %while.12 = (s32[]{:T(128)}, bf16[6,1280,1280]{1,2,0:T(8,128)(2,1)}, f32[6,1280,1]{1,0,2:T(8,128)S(1)}, pred[6,1280]{1,0:T(8,128)(4,1)S(1)}, s32[6,1280]{1,0:T(8...) while((s32[]{:T(128)}, bf16[6,1280,1280]{1,2,0:T(8,128)(2,1)}, ...), condition=%wide.region_12.13_spmd, body=%wide.region_9.12_spmd.sunk | while | flops 444005120 | bytes 23367272 | solution.py:123
  253.4 1.7 fusion.30
  255.1 3.4 fusion.31
  258.5 2.3 fusion.32
  261.0 1.7 fusion.30
  262.7 3.4 fusion.31
  266.1 2.3 fusion.32
  268.7 1.7 fusion.30
  270.4 3.4 fusion.31
  273.9 2.3 fusion.32
  276.4 1.7 fusion.30
  278.1 3.4 fusion.31
  281.5 2.3 fusion.32
  284.1 1.7 fusion.30
  285.8 3.4 fusion.31
  289.2 2.3 fusion.32
  291.7 1.7 fusion.30
  293.5 3.4 fusion.31
  296.8 2.3 fusion.32
  299.3 138.9 %all-to-all-done.2 = bf16[128,128,128]{2,1,0:T(8,128)(2,1)} async-done(((bf16[128,128,128]{2,1,0:T(8,128)(2,1)}), bf16[128,128,128]{2,1,0:T(8,128)(2,1)}, u32[]{:S(2)}, u32[]{:S(2)}) %all-to-all-start.2) | async-done | bytes 4194336 | tf_op jit(solution)/shard_map/all_to_all | solution.py:86
  438.2 4.4 gather_fusion.4
  442.6 11.0 %divide_convert_fusion = bf16[6,1280,128]{2,1,0:T(8,128)(2,1)S(1)} fusion(bf16[6,1280,1280]{1,2,0:T(8,128)(2,1)} %get-tuple-element.49, bf16[6,1280,128]{2,1,0:T(8,128)(2,1)} %bitcast.118, f32[6,1280]{1,0:T(8,128)S(1)} %bitcast.134), kind=kOutput, calls=%fused_computation.22 | convolution fusion | flops 2518548480 | bytes 23623680 | tf_op jit(solution)/shard_map/hqk,hkd->hqd/dot_general | solution.py:131
  453.6 3.1 gather_fusion.5
  456.6 8.9 %all-to-all-start.3 = ((bf16[128,128,128]{2,1,0:T(8,128)(2,1)}), bf16[128,128,128]{2,1,0:T(8,128)(2,1)}, u32[]{:S(2)}, u32[]{:S(2)}) async-start(bf16[128,128,128]{2,1,0:T(8,128)(2,1)} %gather_fusion.5), calls=%async_computation.3 | async-start | bytes 8388608 | tf_op jit(solution)/shard_map/all_to_all | solution.py:135
  465.6 188.1 %all-to-all-done.3 = bf16[128,128,128]{2,1,0:T(8,128)(2,1)} async-done(((bf16[128,128,128]{2,1,0:T(8,128)(2,1)}), bf16[128,128,128]{2,1,0:T(8,128)(2,1)}, u32[]{:S(2)}, u32[]{:S(2)}) %all-to-all-start.3) | async-done | bytes 4194336 | tf_op jit(solution)/shard_map/all_to_all | solution.py:135
  653.7 3.0 gather_fusion.6
  656.9 23.6 %all_to_all.39 = bf16[4,6,2,128,128]{4,3,2,1,0:T(8,128)(2,1)S(1)} all-to-all(bf16[4,6,2,128,128]{4,3,2,1,0:T(8,128)(2,1)S(1)} %copy.77), channel_id=1, replica_groups=mesh['seq'=128,'fsdp'=4] {'fsdp'}, dimensions={0} | all-to-all | bytes 3145728 | tf_op jit(solution)/shard_map/all_to_all | solution.py:141
  680.5 1.1 copy.81
  681.6 2.6 reshape.391
  (81 shorter events, 4.3 us)
Async XLA Ops:
  0.0 7.2 %copy-start = (s32[24,1024]{1,0:T(8,128)S(1)}, s32[24,1024]{1,0:T(8,128)}, u32[]{:S(2)}) copy-start(s32[24,1024]{1,0:T(8,128)} %param.7) | copy-start | bytes 294916
  2.6 7.2 %copy-start.3 = (bf16[256,3072]{1,0:T(8,128)(2,1)S(1)}, bf16[256,3072]{1,0:T(8,128)(2,1)}, u32[]{:S(2)}) copy-start(bf16[256,3072]{1,0:T(8,128)(2,1)} %param.6) | copy-start | bytes 4718596
  2.6 25.3 %all-to-all-start = ((bf16[256,4,768]{0,2,1:T(8,128)(2,1)}), bf16[256,4,768]{0,2,1:T(8,128)(2,1)S(1)}, u32[]{:S(2)}, u32[]{:S(2)}) async-start(bf16[256,4,768]{0,2,1:T(8,128)(2,1)} %bitcast.4), calls=%async_computation | async-start | bytes 3145728 | tf_op jit(solution)/shard_map/all_to_all | solution.py:43
  34.1 207.1 %all-to-all-start.1 = ((bf16[128,128,128]{2,1,0:T(8,128)(2,1)}), bf16[128,128,128]{2,1,0:T(8,128)(2,1)}, u32[]{:S(2)}, u32[]{:S(2)}) async-start(bf16[128,128,128]{2,1,0:T(8,128)(2,1)} %gather_fusion), calls=%async_computation.1 | async-start | bytes 8388608 | tf_op jit(solution)/shard_map/all_to_all | solution.py:83
  53.0 3.4 copy-start.2
  56.7 22.7 %collective-permute-start = (bf16[256,768]{1,0:T(8,128)(2,1)S(1)}, bf16[256,768]{1,0:T(8,128)(2,1)S(1)}, u32[]{:S(2)}, u32[]{:S(2)}) collective-permute-start(bf16[256,768]{1,0:T(8,128)(2,1)S(1)} %bitcast.124), channel_id=1, source_target_pairs={{0,1},{1,2},{2,3},{3,0},{4,5},{5,6},{6,7},{7,4},{8,9},{9,10},{10,1... | collective-permute-start | bytes 1179656 | tf_op jit(solution)/shard_map/ppermute | solution.py:52
  59.4 20.0 %collective-permute-start.1 = (bf16[256,768]{1,0:T(8,128)(2,1)S(1)}, bf16[256,768]{1,0:T(8,128)(2,1)S(1)}, u32[]{:S(2)}, u32[]{:S(2)}) collective-permute-start(bf16[256,768]{1,0:T(8,128)(2,1)S(1)} %bitcast.125), channel_id=1, source_target_pairs={{0,2},{1,3},{2,0},{3,1},{4,6},{5,7},{6,4},{7,5},{8,10},{9,11},{10,... | collective-permute-start | bytes 1179656 | tf_op jit(solution)/shard_map/ppermute | solution.py:52
  63.5 18.6 %collective-permute-start.2 = (bf16[256,768]{1,0:T(8,128)(2,1)S(1)}, bf16[256,768]{1,0:T(8,128)(2,1)S(1)}, u32[]{:S(2)}, u32[]{:S(2)}) collective-permute-start(bf16[256,768]{1,0:T(8,128)(2,1)S(1)} %bitcast.126), channel_id=1, source_target_pairs={{0,3},{1,0},{2,1},{3,2},{4,7},{5,4},{6,5},{7,6},{8,11},{9,8},{10,9... | collective-permute-start | bytes 1179656 | tf_op jit(solution)/shard_map/ppermute | solution.py:52
  82.1 0.7 copy-start.4
  241.2 197.1 %all-to-all-start.2 = ((bf16[128,128,128]{2,1,0:T(8,128)(2,1)}), bf16[128,128,128]{2,1,0:T(8,128)(2,1)}, u32[]{:S(2)}, u32[]{:S(2)}) async-start(bf16[128,128,128]{2,1,0:T(8,128)(2,1)} %gather_fusion.2), calls=%async_computation.2 | async-start | bytes 8388608 | tf_op jit(solution)/shard_map/all_to_all | solution.py:86
  456.6 197.1 %all-to-all-start.3 = ((bf16[128,128,128]{2,1,0:T(8,128)(2,1)}), bf16[128,128,128]{2,1,0:T(8,128)(2,1)}, u32[]{:S(2)}, u32[]{:S(2)}) async-start(bf16[128,128,128]{2,1,0:T(8,128)(2,1)} %gather_fusion.5), calls=%async_computation.3 | async-start | bytes 8388608 | tf_op jit(solution)/shard_map/all_to_all | solution.py:135
  680.5 3.7 copy-start.1
where the time goes:
time: 685 us; the launch traced here: 684 us
  waiting for transfers between devices  508 us (74%)
  starting transfers between devices  50.4 us (7%)
  local copies, waits for them, and re-layouts  40.9 us (6%)
  other arithmetic  39.3 us (6%)
  blocking collectives  23.6 us (3%)
  matrix products  21.4 us (3%)
    all_to_all x1, waiting for transfers between devices, shards(): lax.all_to_all(by_index(outputs, back_pick), 'seq', split_axis=0, concat_...  188 us
    all_to_all x1, waiting for transfers between devices, shards(): lax.all_to_all(key_send, 'seq', split_axis=0, concat_axis=0, tiled=True)  151 us
    all_to_all x1, waiting for transfers between devices, shards(): lax.all_to_all(value_send, 'seq', split_axis=0, concat_axis=0, tiled=True)  139 us
    all_to_all x1, blocking collectives, shards(): lax.all_to_all(jnp.swapaxes(own_output, 0, 1), 'fsdp', split_axis=0, conc...  23.6 us
    dynamic_update_slice x12, other arithmetic, shards(): lax.map(one_head, (key_grouped.reshape(group_heads, group_rows, head_dim)...  20.4 us
    gather x6, local copies, waits for them, and re-layouts, by_index(): return source_table[jnp.clip(row_index, 0, source_table.shape[0] - 1)]  19.8 us
    all_to_all x1, starting transfers between devices, shards(): lax.all_to_all(key_send, 'seq', split_axis=0, concat_axis=0, tiled=True)  18.9 us
    all_to_all x1, waiting for transfers between devices, shards(): lax.all_to_all(query_key, 'fsdp', split_axis=1, concat_axis=0, tiled=True)  16.1 us
  transfers between devices with their start and end apart: 7, of which 6 were waited for; matrix products, arithmetic and copies ran while one was open for 10% of the time, Pallas kernels for 0%

commit v1 on v0

--- a/solution.py
+++ b/solution.py
@@ -40,7 +40,12 @@
     send_rows = seq_count * slot_count
     score_scale = 1.0 / math.sqrt(head_dim)
     own_blocks = tok_rows // BLK
-    keys_local = lax.all_to_all(query_key, "fsdp", split_axis=1, concat_axis=0, tiled=True)
+    keys_local = jnp.concatenate(
+        lax.all_to_all(
+            jnp.stack(jnp.split(query_key, lax.axis_size("fsdp"), axis=1)), "fsdp", 0, 0
+        ),
+        axis=0,
+    )
     value_chunks = values.reshape(tok_rows, group_count, group_heads * head_dim)
     value_chunks, keys_local = lax.optimization_barrier((value_chunks, keys_local))
     by_shift = [lax.dynamic_index_in_dim(value_chunks, group_index, 1, keepdims=False)]

time: 685 us -> 687 us (level)
  no operation moved by 1% of the time
where the time goes in v1:
time: 687 us; the launch traced here: 686 us
  waiting for transfers between devices  508 us (74%)
  starting transfers between devices  50.4 us (7%)
  local copies, waits for them, and re-layouts  41.2 us (6%)
  other arithmetic  40.6 us (6%)
  blocking collectives  23.6 us (3%)
  matrix products  21.4 us (3%)
    all_to_all x1, waiting for transfers between devices, shards(): lax.all_to_all(by_index(outputs, back_pick), 'seq', split_axis=0, concat_...  188 us
    all_to_all x1, waiting for transfers between devices, shards(): lax.all_to_all(key_send, 'seq', split_axis=0, concat_axis=0, tiled=True)  151 us
    all_to_all x1, waiting for transfers between devices, shards(): lax.all_to_all(value_send, 'seq', split_axis=0, concat_axis=0, tiled=True)  139 us
    all_to_all x1, blocking collectives, shards(): lax.all_to_all(jnp.swapaxes(own_output, 0, 1), 'fsdp', split_axis=0, conc...  23.6 us
    dynamic_update_slice x12, other arithmetic, shards(): lax.map(one_head, (key_grouped.reshape(group_heads, group_rows, head_dim)...  20.4 us
    gather x6, local copies, waits for them, and re-layouts, by_index(): return source_table[jnp.clip(row_index, 0, source_table.shape[0] - 1)]  19.8 us
    all_to_all x1, starting transfers between devices, shards(): lax.all_to_all(key_send, 'seq', split_axis=0, concat_axis=0, tiled=True)  18.9 us
    all_to_all x1, waiting for transfers between devices, shards(): lax.all_to_all(jnp.stack(jnp.split(query_key, lax.axis_size('fsdp'), axis...  16.1 us
  transfers between devices with their start and end apart: 7, of which 6 were waited for; matrix products, arithmetic and copies ran while one was open for 10% of the time, Pallas kernels for 0%

profile of v1, /device:TPU:70, one launch (start us, length us, event | category | flops | bytes accessed | tf_op | source)
XLA Modules:
  0.0 685.8 jit_solution(1297610700516449343)
XLA Ops:
  0.0 1.5 slice_bitcast_fusion.3
  1.5 1.3 pad_maximum_fusion
  2.8 4.6 all-to-all-start
  7.5 1.0 reshape.314
  8.4 1.1 copy.58
  9.5 0.2 dynamic-slice_reduce_fusion.2
  9.7 0.2 convert_reduce_fusion
  10.0 1.6 copy.55
  12.0 16.1 %all-to-all-done = bf16[4,256,768]{2,1,0:T(8,128)(2,1)S(1)} async-done(((bf16[4,256,768]{2,1,0:T(8,128)(2,1)}), bf16[4,256,768]{2,1,0:T(8,128)(2,1)S(1)}, u32[]{:S(2)}, u32[]{:S(2)}) %all-to-all-start) | async-done | bytes 1572896 | tf_op jit(solution)/shard_map/all_to_all | solution.py:44
  28.2 0.7 copy.56
  28.9 1.6 copy.80
  30.5 2.1 copy.57
  32.6 3.1 gather_fusion
  35.7 18.9 %all-to-all-start.1 = ((bf16[128,128,128]{2,1,0:T(8,128)(2,1)}), bf16[128,128,128]{2,1,0:T(8,128)(2,1)}, u32[]{:S(2)}, u32[]{:S(2)}) async-start(bf16[128,128,128]{2,1,0:T(8,128)(2,1)} %gather_fusion), calls=%async_computation.1 | async-start | bytes 8388608 | tf_op jit(solution)/shard_map/all_to_all | solution.py:88
  54.9 0.2 reshape.335
  55.5 0.2 broadcast_in_dim.121
  55.8 1.7 reduce-window.6
  57.5 0.2 slice_reduce_fusion
  58.4 2.5 collective-permute-start
  61.0 4.0 collective-permute-start.1
  65.2 2.5 collective-permute-start.2
  67.9 0.6 select_reduce_fusion
  68.7 0.3 fusion.9
  69.5 11.5 %collective-permute-done = bf16[256,768]{1,0:T(8,128)(2,1)S(1)} collective-permute-done((bf16[256,768]{1,0:T(8,128)(2,1)S(1)}, bf16[256,768]{1,0:T(8,128)(2,1)S(1)}, u32[]{:S(2)}, u32[]{:S(2)}) %collective-permute-start) | collective-permute-done | bytes 393248 | tf_op jit(solution)/shard_map/ppermute | solution.py:57
  81.1 2.7 collective-permute-done.2
  83.8 0.7 copy-done.4
  84.5 1.2 pad_maximum_fusion.1
  85.7 0.6 gather_fusion.1
  86.4 1.0 copy.66
  87.4 0.6 reshape_reshape.4
  88.1 1.1 copy.67
  89.2 3.1 gather_fusion.2
  92.3 150.5 %all-to-all-done.1 = bf16[128,128,128]{2,1,0:T(8,128)(2,1)} async-done(((bf16[128,128,128]{2,1,0:T(8,128)(2,1)}), bf16[128,128,128]{2,1,0:T(8,128)(2,1)}, u32[]{:S(2)}, u32[]{:S(2)}) %all-to-all-start.1) | async-done | bytes 4194336 | tf_op jit(solution)/shard_map/all_to_all | solution.py:88
  242.8 9.0 %all-to-all-start.2 = ((bf16[128,128,128]{2,1,0:T(8,128)(2,1)}), bf16[128,128,128]{2,1,0:T(8,128)(2,1)}, u32[]{:S(2)}, u32[]{:S(2)}) async-start(bf16[128,128,128]{2,1,0:T(8,128)(2,1)} %gather_fusion.2), calls=%async_computation.2 | async-start | bytes 8388608 | tf_op jit(solution)/shard_map/all_to_all | solution.py:91
  251.8 3.1 gather_fusion.3
  254.9 46.0 %while.12 = (s32[]{:T(128)}, bf16[6,1280,1280]{1,2,0:T(8,128)(2,1)}, f32[6,1280,1]{1,0,2:T(8,128)S(1)}, pred[6,1280]{1,0:T(8,128)(4,1)S(1)}, s32[6,1280]{1,0:T(8...) while((s32[]{:T(128)}, bf16[6,1280,1280]{1,2,0:T(8,128)(2,1)}, ...), condition=%wide.region_12.13_spmd, body=%wide.region_9.12_spmd.sunk | while | flops 444005120 | bytes 23367272 | solution.py:128
  255.0 1.7 fusion.30
  256.8 3.4 fusion.31
  260.1 2.3 fusion.32
  262.7 1.7 fusion.30
  264.4 3.4 fusion.31
  267.8 2.3 fusion.32
  270.4 1.7 fusion.30
  272.1 3.4 fusion.31
  275.5 2.3 fusion.32
  278.1 1.7 fusion.30
  279.8 3.4 fusion.31
  283.2 2.3 fusion.32
  285.7 1.7 fusion.30
  287.5 3.4 fusion.31
  290.9 2.3 fusion.32
  293.4 1.7 fusion.30
  295.1 3.4 fusion.31
  298.5 2.3 fusion.32
  301.0 138.9 %all-to-all-done.2 = bf16[128,128,128]{2,1,0:T(8,128)(2,1)} async-done(((bf16[128,128,128]{2,1,0:T(8,128)(2,1)}), bf16[128,128,128]{2,1,0:T(8,128)(2,1)}, u32[]{:S(2)}, u32[]{:S(2)}) %all-to-all-start.2) | async-done | bytes 4194336 | tf_op jit(solution)/shard_map/all_to_all | solution.py:91
  439.9 4.4 gather_fusion.4
  444.3 11.0 %divide_convert_fusion = bf16[6,1280,128]{2,1,0:T(8,128)(2,1)S(1)} fusion(bf16[6,1280,1280]{1,2,0:T(8,128)(2,1)} %get-tuple-element.49, bf16[6,1280,128]{2,1,0:T(8,128)(2,1)} %bitcast.123, f32[6,1280]{1,0:T(8,128)S(1)} %bitcast.139), kind=kOutput, calls=%fused_computation.22 | convolution fusion | flops 2518548480 | bytes 23623680 | tf_op jit(solution)/shard_map/hqk,hkd->hqd/dot_general | solution.py:136
  455.2 3.1 gather_fusion.5
  458.3 8.9 %all-to-all-start.3 = ((bf16[128,128,128]{2,1,0:T(8,128)(2,1)}), bf16[128,128,128]{2,1,0:T(8,128)(2,1)}, u32[]{:S(2)}, u32[]{:S(2)}) async-start(bf16[128,128,128]{2,1,0:T(8,128)(2,1)} %gather_fusion.5), calls=%async_computation.3 | async-start | bytes 8388608 | tf_op jit(solution)/shard_map/all_to_all | solution.py:140
  467.3 188.1 %all-to-all-done.3 = bf16[128,128,128]{2,1,0:T(8,128)(2,1)} async-done(((bf16[128,128,128]{2,1,0:T(8,128)(2,1)}), bf16[128,128,128]{2,1,0:T(8,128)(2,1)}, u32[]{:S(2)}, u32[]{:S(2)}) %all-to-all-start.3) | async-done | bytes 4194336 | tf_op jit(solution)/shard_map/all_to_all | solution.py:140
  655.4 3.0 gather_fusion.6
  658.6 23.6 %all_to_all.25 = bf16[4,6,2,128,128]{4,3,2,1,0:T(8,128)(2,1)S(1)} all-to-all(bf16[4,6,2,128,128]{4,3,2,1,0:T(8,128)(2,1)S(1)} %copy.71), channel_id=1, replica_groups=mesh['seq'=128,'fsdp'=4] {'fsdp'}, dimensions={0} | all-to-all | bytes 3145728 | tf_op jit(solution)/shard_map/all_to_all | solution.py:146
  682.1 1.1 copy.75
  683.2 2.6 reshape.392
  (81 shorter events, 4.3 us)
Async XLA Ops:
  0.0 7.4 %copy-start = (s32[24,1024]{1,0:T(8,128)S(1)}, s32[24,1024]{1,0:T(8,128)}, u32[]{:S(2)}) copy-start(s32[24,1024]{1,0:T(8,128)} %param.7) | copy-start | bytes 294916
  2.8 7.2 %copy-start.3 = (bf16[256,3072]{1,0:T(8,128)(2,1)S(1)}, bf16[256,3072]{1,0:T(8,128)(2,1)}, u32[]{:S(2)}) copy-start(bf16[256,3072]{1,0:T(8,128)(2,1)} %param.6) | copy-start | bytes 4718596
  2.8 25.3 %all-to-all-start = ((bf16[4,256,768]{2,1,0:T(8,128)(2,1)}), bf16[4,256,768]{2,1,0:T(8,128)(2,1)S(1)}, u32[]{:S(2)}, u32[]{:S(2)}) async-start(bf16[4,256,768]{2,1,0:T(8,128)(2,1)} %pad_maximum_fusion), calls=%async_computation | async-start | bytes 3145728 | tf_op jit(solution)/shard_map/all_to_all | solution.py:44
  35.7 207.1 %all-to-all-start.1 = ((bf16[128,128,128]{2,1,0:T(8,128)(2,1)}), bf16[128,128,128]{2,1,0:T(8,128)(2,1)}, u32[]{:S(2)}, u32[]{:S(2)}) async-start(bf16[128,128,128]{2,1,0:T(8,128)(2,1)} %gather_fusion), calls=%async_computation.1 | async-start | bytes 8388608 | tf_op jit(solution)/shard_map/all_to_all | solution.py:88
  54.7 3.4 copy-start.2
  58.4 22.7 %collective-permute-start = (bf16[256,768]{1,0:T(8,128)(2,1)S(1)}, bf16[256,768]{1,0:T(8,128)(2,1)S(1)}, u32[]{:S(2)}, u32[]{:S(2)}) collective-permute-start(bf16[256,768]{1,0:T(8,128)(2,1)S(1)} %bitcast.129), channel_id=1, source_target_pairs={{0,1},{1,2},{2,3},{3,0},{4,5},{5,6},{6,7},{7,4},{8,9},{9,10},{10,1... | collective-permute-start | bytes 1179656 | tf_op jit(solution)/shard_map/ppermute | solution.py:57
  61.0 20.0 %collective-permute-start.1 = (bf16[256,768]{1,0:T(8,128)(2,1)S(1)}, bf16[256,768]{1,0:T(8,128)(2,1)S(1)}, u32[]{:S(2)}, u32[]{:S(2)}) collective-permute-start(bf16[256,768]{1,0:T(8,128)(2,1)S(1)} %bitcast.130), channel_id=1, source_target_pairs={{0,2},{1,3},{2,0},{3,1},{4,6},{5,7},{6,4},{7,5},{8,10},{9,11},{10,... | collective-permute-start | bytes 1179656 | tf_op jit(solution)/shard_map/ppermute | solution.py:57
  65.2 18.6 %collective-permute-start.2 = (bf16[256,768]{1,0:T(8,128)(2,1)S(1)}, bf16[256,768]{1,0:T(8,128)(2,1)S(1)}, u32[]{:S(2)}, u32[]{:S(2)}) collective-permute-start(bf16[256,768]{1,0:T(8,128)(2,1)S(1)} %bitcast.131), channel_id=1, source_target_pairs={{0,3},{1,0},{2,1},{3,2},{4,7},{5,4},{6,5},{7,6},{8,11},{9,8},{10,9... | collective-permute-start | bytes 1179656 | tf_op jit(solution)/shard_map/ppermute | solution.py:57
  83.8 0.7 copy-start.4
  242.8 197.1 %all-to-all-start.2 = ((bf16[128,128,128]{2,1,0:T(8,128)(2,1)}), bf16[128,128,128]{2,1,0:T(8,128)(2,1)}, u32[]{:S(2)}, u32[]{:S(2)}) async-start(bf16[128,128,128]{2,1,0:T(8,128)(2,1)} %gather_fusion.2), calls=%async_computation.2 | async-start | bytes 8388608 | tf_op jit(solution)/shard_map/all_to_all | solution.py:91
  458.3 197.1 %all-to-all-start.3 = ((bf16[128,128,128]{2,1,0:T(8,128)(2,1)}), bf16[128,128,128]{2,1,0:T(8,128)(2,1)}, u32[]{:S(2)}, u32[]{:S(2)}) async-start(bf16[128,128,128]{2,1,0:T(8,128)(2,1)} %gather_fusion.5), calls=%async_computation.3 | async-start | bytes 8388608 | tf_op jit(solution)/shard_map/all_to_all | solution.py:140
  682.1 3.7 copy-start.1
